TPU v7x, 256 devices: a whole 4x4x8 slice. The times are simulated.
256 devices in a mesh: dp: 4 (over z_hi), expert: 16 (over y, z_lo, core), mp: 4 (over x).
Axes of the slice: x: 4, y: 4, z: 8 (z_hi: 4, z_lo: 2; z = z_hi * 2 + z_lo), core: 2. Of those that a mesh axis runs over, the one named last changes fastest.
Arguments:
- hidden: bfloat16 [16384, 2048], P(('dp', 'expert', 'mp')), may hold values from -6 to 6
- norm_gain: float32 [2048], replicated, may hold values from 0.1 to 1.9
- expert_in: float32 [64, 2048, 2816], P('dp', ('expert', 'mp')), may hold values from -0.125 to 0.125
- expert_out: float32 [64, 2048, 1408], P('dp', ('expert', 'mp')), may hold values from -0.15625 to 0.15625
- expert_ids: int32 [16384, 6], P(('dp', 'expert', 'mp')), may hold values from 0 to 63, all different within a row; in each aligned block of 64 rows (0 to 63, 64 to 127, ...) at most 12 rows name the same one
- gate_levels: int32 [16384, 6], P(('dp', 'expert', 'mp')), may hold values from 1 to 255
- shared_gate: bfloat16 [2048, 2816], P(('dp', 'expert'), 'mp'), may hold values from -0.125 to 0.125
- shared_up: bfloat16 [2048, 2816], P(('dp', 'expert'), 'mp'), may hold values from -0.125 to 0.125
- shared_down: bfloat16 [2048, 2816], P(('dp', 'expert'), 'mp'), may hold values from -0.109375 to 0.109375
- next_gain: float32 [2048], replicated, may hold values from 0.1 to 1.9
- kv_weight: bfloat16 [2048, 576], P(None, 'mp'), may hold values from -0.125 to 0.125
Outputs:
- layer_out: bfloat16 [16384, 2048], P(('dp', 'expert', 'mp'))
- kv_latent: bfloat16 [16384, 576], P(('dp', 'expert'), 'mp')
Inputs may be any that keep to these rules, and one draw needn't show every extreme that they name: `expert_ids`: each row names 6 different experts. Among the 64 rows of one device no expert is named by more than 12 rows, and in every draw some expert is named by exactly 12 rows of some device.
All inputs are finite; a program needn't handle non-finite values.
Results may differ from a plain program's by a relative error of at most 0.012.
Values may be sent and summed in bfloat16 or wider, within the bound.
No kernel may reach another device: no remote copies, remote signals or barrier semaphores. Data moves between devices by JAX's collectives and lax.ppermute only.
A program may use at most 128 MiB of HBM per device.

v0:
```python
import jax
import jax.numpy as jnp
from jax import lax
from jax.sharding import PartitionSpec as P


def rms_scale(values, gain):
    wide = values.astype(jnp.float32)
    mean_sq = jnp.mean(wide * wide, axis=-1, keepdims=True)
    return (wide * lax.rsqrt(mean_sq + 1e-06) * gain).astype(jnp.bfloat16)


def expert_part(rows, gate_up_w, down_w):
    quarter = down_w.shape[1]
    gate_up = jnp.dot(rows, gate_up_w, preferred_element_type=jnp.float32)
    act = (jax.nn.silu(gate_up[:, :quarter]) * gate_up[:, quarter:]).astype(jnp.bfloat16)
    return lax.dot_general(
        act, down_w, (((1,), (1,)), ((), ())), preferred_element_type=jnp.float32
    )


def on_device(
    hidden,
    norm_gain,
    expert_in,
    expert_out,
    expert_ids,
    gate_levels,
    shared_gate,
    shared_up,
    shared_down,
    next_gain,
    kv_weight,
):
    tok_rows, width = hidden.shape
    top = expert_ids.shape[1]
    n_mp = lax.axis_size("mp")
    n_groups = lax.axis_size(("dp", "expert"))
    capacity = min(tok_rows, (2 * tok_rows * top + n_groups - 1) // n_groups)
    local_e, local_rows, double = expert_in.shape
    full_ff = double // 2
    quarter = full_ff // n_mp
    in_cast = (
        expert_in.astype(jnp.bfloat16)
        .reshape(local_e, local_rows, 2, n_mp, quarter)
        .transpose(0, 3, 1, 2, 4)
    )
    out_cast = (
        expert_out.astype(jnp.bfloat16)
        .reshape(local_e, local_rows, n_mp, quarter)
        .transpose(0, 2, 1, 3)
    )
    in_send = in_cast.reshape(local_e * n_mp, local_rows, 2, quarter)
    out_send = out_cast.reshape(local_e * n_mp, local_rows, quarter)
    in_recv, out_recv = (
        lax.all_to_all(in_send, ("expert", "mp"), split_axis=0, concat_axis=1, tiled=True),
        lax.all_to_all(out_send, ("expert", "mp"), split_axis=0, concat_axis=1, tiled=True),
    )
    gate_up_w = in_recv.reshape(width, 2 * quarter)
    down_w = out_recv.reshape(width, quarter)
    normed = rms_scale(hidden, norm_gain)
    levels = gate_levels.astype(jnp.float32)
    gate_weights = levels / jnp.sum(levels, axis=1, keepdims=True)
    flat_ids = expert_ids.reshape(-1)
    pairs = flat_ids.shape[0]
    onehot = (flat_ids[:, None] == jnp.arange(n_groups, dtype=jnp.int32)[None, :]).astype(jnp.int32)
    before = jnp.cumsum(onehot, axis=0) - onehot
    slot_of_pair = jnp.sum(before * onehot, axis=1)
    target = flat_ids * capacity + slot_of_pair
    token_of_pair = jnp.arange(pairs, dtype=jnp.int32) // top
    send = (
        jnp.zeros((n_groups * capacity, width), jnp.bfloat16).at[target].set(normed[token_of_pair])
    )
    received = lax.all_to_all(
        send.reshape(n_groups, capacity, width),
        ("dp", "expert"),
        split_axis=0,
        concat_axis=0,
        tiled=True,
    )
    slots_here = received.reshape(n_groups * capacity, width)
    every_slot = lax.all_gather(slots_here, "mp", axis=0, tiled=True)
    rows = every_slot
    summed = lax.psum_scatter(
        expert_part(rows, gate_up_w, down_w).astype(jnp.bfloat16),
        "mp",
        scatter_dimension=0,
        tiled=True,
    )
    result = summed.reshape(n_groups, capacity, width)
    back = lax.all_to_all(
        result, ("dp", "expert"), split_axis=0, concat_axis=0, tiled=True
    ).reshape(n_groups * capacity, width)
    picked = back[target].reshape(tok_rows, top, width)
    routed = jnp.sum(picked.astype(jnp.float32) * gate_weights[:, :, None], axis=1)
    shared_cols = shared_gate.shape[1]
    shared_cat = jnp.concatenate([shared_gate, shared_up, shared_down], axis=1)
    shared_cat = lax.all_gather(shared_cat, "dp", axis=0, tiled=False)
    shared_cat = lax.all_gather(shared_cat, "expert", axis=1, tiled=False)
    shared_cat = shared_cat.reshape(width, 3 * shared_cols)
    gate_w = shared_cat[:, :shared_cols]
    up_w = shared_cat[:, shared_cols : 2 * shared_cols]
    down_s = shared_cat[:, 2 * shared_cols :]
    group_rows = lax.all_gather(normed, "mp", axis=0, tiled=True)
    rows = group_rows
    gate_part = jnp.dot(rows, gate_w, preferred_element_type=jnp.float32)
    up_part = jnp.dot(rows, up_w, preferred_element_type=jnp.float32)
    act = (jax.nn.silu(gate_part) * up_part).astype(jnp.bfloat16)
    shared_out = lax.psum_scatter(
        lax.dot_general(act, down_s, (((1,), (1,)), ((), ())), preferred_element_type=jnp.float32),
        "mp",
        scatter_dimension=0,
        tiled=True,
    )
    layer_out = (hidden.astype(jnp.float32) + routed + shared_out).astype(jnp.bfloat16)
    next_rows = rms_scale(layer_out, next_gain)
    next_group = lax.all_gather(next_rows, "mp", axis=0, tiled=True)
    kv_latent = jnp.dot(next_group, kv_weight, preferred_element_type=jnp.float32).astype(
        jnp.bfloat16
    )
    return (layer_out, kv_latent)


def solution(mesh):
    in_specs = (
        P(("dp", "expert", "mp"), None),
        P(),
        P("dp", ("expert", "mp"), None),
        P("dp", ("expert", "mp"), None),
        P(("dp", "expert", "mp"), None),
        P(("dp", "expert", "mp"), None),
        P(("dp", "expert"), "mp"),
        P(("dp", "expert"), "mp"),
        P(("dp", "expert"), "mp"),
        P(),
        P(None, "mp"),
    )
    out_specs = (P(("dp", "expert", "mp"), None), P(("dp", "expert"), "mp"))
    return jax.shard_map(
        on_device, mesh=mesh, in_specs=in_specs, out_specs=out_specs, check_vma=False
    )
```

profile of v0, /device:TPU:1, one launch (start us, length us, event | category | flops | bytes accessed | tf_op | source)
XLA Modules:
  0.0 692.3 jit_solution(3124470099262172469)
XLA Ops:
  12.9 10.0 %scatter_custom_fusion = bf16[768,2048]{1,0:T(8,128)(2,1)} fusion(s32[384]{0:T(512)S(1)} %fusion.38, bf16[64,2048]{1,0:T(8,128)(2,1)S(1)} %fusion.30, s32[1024]{0:T(1024)S(1)} %pad_clamp_fusion.1, bf16[]{:T(256)} %constant.12.clone.1), kind=kCustom, calls=%fused_computation.15 | custom fusion | bytes 3145730 | tf_op jit(solution)/shard_map/scatter | solution.py:72
  22.8 6.1 reshape.156
  28.9 108.9 %all_to_all.28 = bf16[64,12,2048]{2,1,0:T(8,128)(2,1)} all-to-all(bf16[64,12,2048]{2,1,0:T(8,128)(2,1)} %reshape.156), channel_id=1, replica_groups=mesh['dp'=4,'expert'=16,'mp'=4] {'dp','expert'}, dimensions={0} | all-to-all | bytes 6291456 | tf_op jit(solution)/shard_map/all_to_all | solution.py:74
  137.8 6.2 reshape.157
  147.0 5.1 reshape.158
  152.1 4.8 copy.24
  156.9 9.3 %all-to-all-start.1 = ((bf16[64,32,2,352]{3,1,2,0:T(8,128)(2,1)}), bf16[64,32,2,352]{3,1,2,0:T(8,128)(2,1)}, u32[]{:S(2)}, u32[]{:S(2)}) async-start(bf16[64,32,2,352]{3,1,2,0:T(8,128)(2,1)} %bitcast.33), calls=%async_computation.1 | async-start | bytes 6291456 | tf_op jit(solution)/shard_map/all_to_all | solution.py:56
  168.3 54.8 %all-to-all-done.1 = bf16[64,32,2,352]{3,1,2,0:T(8,128)(2,1)} async-done(((bf16[64,32,2,352]{3,1,2,0:T(8,128)(2,1)}), bf16[64,32,2,352]{3,1,2,0:T(8,128)(2,1)}, u32[]{:S(2)}, u32[]{:S(2)}) %all-to-all-start.1) | async-done | bytes 2883616 | tf_op jit(solution)/shard_map/all_to_all | solution.py:56
  227.5 6.9 copy.25
  234.4 7.8 %reshape.160 = bf16[2048,704]{1,0:T(8,128)(2,1)} reshape(bf16[64,32,2,352]{3,2,1,0:T(2,128)(2,1)} %copy.25) | data formatting | bytes 5767168 | tf_op jit(solution)/shard_map/reshape | solution.py:59
  242.2 70.8 %all-gather.7.cloned.1.call-done = bf16[3072,2048]{1,0:T(8,128)(2,1)} async-done(((bf16[768,2048]{1,0:T(8,128)(2,1)}), bf16[3072,2048]{1,0:T(8,128)(2,1)}) %all-gather.7.cloned.1.call-update) | async-done | bytes 12582928 | tf_op jit(solution)/shard_map/all_gather | solution.py:82
  312.9 15.1 %fusion.44 = f32[3072,704]{0,1:T(8,128)} fusion(bf16[3072,2048]{1,0:T(8,128)(2,1)} %all-gather.7.cloned.1.call-done, bf16[2048,704]{1,0:T(8,128)(2,1)} %reshape.160), kind=kOutput, calls=%fused_computation.67 | convolution fusion | flops 8858370048 | bytes 24117248 | tf_op jit(solution)/shard_map/dot_general | solution.py:15
  328.1 13.5 %convolution_convert_fusion = bf16[3072,2048]{1,0:T(8,128)(2,1)} fusion(bf16[2048,352]{1,0:T(8,128)(2,1)S(1)} %bitcast.36, f32[3072,704]{0,1:T(8,128)} %fusion.44), kind=kOutput, calls=%fused_computation.3 | convolution fusion | flops 4441964544 | bytes 22675456 | tf_op jit(solution)/shard_map/dot_general | solution.py:17
  342.5 17.1 %all-gather = bf16[128,2112]{1,0:T(8,128)(2,1)} all-gather(bf16[32,2112]{1,0:T(8,128)(2,1)S(1)} %concatenate.7), channel_id=2, replica_groups=mesh['dp'=4,'expert'=16,'mp'=4] {'dp'}, dimensions={0}, use_global_device_ids=true | all-gather | bytes 675840 | tf_op jit(solution)/shard_map/all_gather | solution.py:98
  359.7 100.2 %reduce-scatter.3.cloned.1.call-done = bf16[768,2048]{1,0:T(8,128)(2,1)} async-done(((bf16[3072,2048]{1,0:T(8,128)(2,1)}), bf16[768,2048]{1,0:T(8,128)(2,1)}) %reduce-scatter.3.cloned.1.call-update) | async-done | bytes 3145744 | tf_op jit(solution)/shard_map/reduce_scatter | solution.py:84
  459.9 6.1 reshape.163
  466.0 10.8 %all-to-all-start.3 = ((bf16[64,12,2048]{2,1,0:T(8,128)(2,1)}), bf16[64,12,2048]{2,1,0:T(8,128)(2,1)}, u32[]{:S(2)}, u32[]{:S(2)}) async-start(bf16[64,12,2048]{2,1,0:T(8,128)(2,1)} %reshape.163), calls=%async_computation.4 | async-start | bytes 8388608 | tf_op jit(solution)/shard_map/all_to_all | solution.py:91
  477.1 10.5 %all-gather.9.cloned.1.call-done = bf16[256,2048]{1,0:T(8,128)(2,1)} async-done(((bf16[64,2048]{1,0:T(8,128)(2,1)}), bf16[256,2048]{1,0:T(8,128)(2,1)}) %all-gather.9.cloned.1.call-update) | async-done | bytes 1048592 | tf_op jit(solution)/shard_map/all_gather | solution.py:104
  487.6 125.0 %all-gather.13.cloned.1.call-done = bf16[4,512,2112]{2,1,0:T(8,128)(2,1)} async-done(((bf16[4,32,2112]{2,1,0:T(8,128)(2,1)}), bf16[4,512,2112]{2,1,0:T(8,128)(2,1)}) %all-gather.13.cloned.1.call-update) | async-done | bytes 8650768 | tf_op jit(solution)/shard_map/all_gather | solution.py:99
  616.2 8.8 %fusion.1 = f32[256,2048]{1,0:T(8,128)} fusion(bf16[2048,2112]{1,0:T(8,128)(2,1)} %bitcast.39, bf16[256,2048]{1,0:T(8,128)(2,1)S(1)} %copy-done.10, f32[256,704]{0,1:T(8,128)S(1)} %fusion.5), kind=kOutput, calls=%fused_computation.7 | convolution fusion | flops 1477476352 | bytes 10158080 | tf_op jit(solution)/shard_map/dot_general | solution.py:110
  625.1 6.2 reshape.164
  631.3 6.7 gather_fusion
  644.0 11.2 %reduce-scatter.5.cloned.1.call-done = f32[64,2048]{1,0:T(8,128)} async-done(((f32[256,2048]{1,0:T(8,128)}), f32[64,2048]{1,0:T(8,128)}) %reduce-scatter.5.cloned.1.call-update) | async-done | bytes 524304 | tf_op jit(solution)/shard_map/reduce_scatter | solution.py:109
  657.4 25.5 %all-gather.11.cloned.1.call-done = bf16[256,2048]{1,0:T(8,128)(2,1)} async-done(((bf16[64,2048]{1,0:T(8,128)(2,1)}), bf16[256,2048]{1,0:T(8,128)(2,1)}) %all-gather.11.cloned.1.call-update) | async-done | bytes 1048592 | tf_op jit(solution)/shard_map/all_gather | solution.py:117
  (70 shorter events, 30.5 us)
Async XLA Ops:
  7.2 675.7 %copy-start = (bf16[2048,144]{0,1:T(8,128)(2,1)S(1)}, bf16[2048,144]{0,1:T(8,128)(2,1)}, u32[]{:S(2)}) copy-start(bf16[2048,144]{0,1:T(8,128)(2,1)} %param.21) | copy-start | bytes 1769476
  7.2 305.8 %all-gather.7.cloned.1.call-start = ((), (), s32[]{:S(2)}) async-start(), calls=%async_computation.6 | async-start | bytes 15728640 | tf_op jit(solution)/shard_map/all_gather | solution.py:82
  12.9 16.1 %copy-start.3 = (bf16[64,2048]{1,0:T(8,128)(2,1)}, bf16[64,2048]{1,0:T(8,128)(2,1)S(1)}, u32[]{:S(2)}) copy-start(bf16[64,2048]{1,0:T(8,128)(2,1)S(1)} %fusion.30) | copy-start | bytes 786436
  156.9 9.3 %copy-start.1 = (f32[16,32,1408]{2,1,0:T(8,128)S(1)}, f32[16,32,1408]{2,1,0:T(8,128)}, u32[]{:S(2)}) copy-start(f32[16,32,1408]{2,1,0:T(8,128)} %param.14) | copy-start | bytes 8650756
  156.9 66.2 %all-to-all-start.1 = ((bf16[64,32,2,352]{3,1,2,0:T(8,128)(2,1)}), bf16[64,32,2,352]{3,1,2,0:T(8,128)(2,1)}, u32[]{:S(2)}, u32[]{:S(2)}) async-start(bf16[64,32,2,352]{3,1,2,0:T(8,128)(2,1)} %bitcast.33), calls=%async_computation.1 | async-start | bytes 6291456 | tf_op jit(solution)/shard_map/all_to_all | solution.py:56
  223.1 105.0 %all-to-all-start.2 = ((bf16[64,32,352]{2,1,0:T(8,128)(2,1)}), bf16[64,32,352]{2,1,0:T(8,128)(2,1)S(1)}, u32[]{:S(2)}, u32[]{:S(2)}) async-start(bf16[64,32,352]{2,1,0:T(8,128)(2,1)} %bitcast.3), calls=%async_computation.2 | async-start | bytes 3145728 | tf_op jit(solution)/shard_map/all_to_all | solution.py:57
  227.4 232.4 %reduce-scatter.3.cloned.1.call-start = ((), (), s32[]{:S(2)}) async-start(), calls=%async_computation.7 | async-start | bytes 15728640 | tf_op jit(solution)/shard_map/reduce_scatter | solution.py:84
  341.6 0.8 copy-start.5
  341.6 0.8 copy-start.6
  341.6 0.8 copy-start.7
  341.6 146.0 %all-gather.9.cloned.1.call-start = ((), (), s32[]{:S(2)}) async-start(), calls=%async_computation.8 | async-start | bytes 1310720 | tf_op jit(solution)/shard_map/all_gather | solution.py:104
  342.3 270.3 %all-gather.13.cloned.1.call-start = ((), (), s32[]{:S(2)}) async-start(), calls=%async_computation.11 | async-start | bytes 9469952 | tf_op jit(solution)/shard_map/all_gather | solution.py:99
  466.0 159.2 %all-to-all-start.3 = ((bf16[64,12,2048]{2,1,0:T(8,128)(2,1)}), bf16[64,12,2048]{2,1,0:T(8,128)(2,1)}, u32[]{:S(2)}, u32[]{:S(2)}) async-start(bf16[64,12,2048]{2,1,0:T(8,128)(2,1)} %reshape.163), calls=%async_computation.4 | async-start | bytes 8388608 | tf_op jit(solution)/shard_map/all_to_all | solution.py:91
  476.8 178.4 %reduce-scatter.5.cloned.1.call-start = ((), (), s32[]{:S(2)}) async-start(), calls=%async_computation.9 | async-start | bytes 2621440 | tf_op jit(solution)/shard_map/reduce_scatter | solution.py:109
  487.6 128.5 %copy-start.10 = (bf16[256,2048]{1,0:T(8,128)(2,1)S(1)}, bf16[256,2048]{1,0:T(8,128)(2,1)}, u32[]{:S(2)}) copy-start(bf16[256,2048]{1,0:T(8,128)(2,1)} %all-gather.9.cloned.1.call-done) | copy-start | bytes 3145732
  616.1 8.8 %copy-start.8 = (s32[64,6]{0,1:T(8,128)S(1)}, s32[64,6]{0,1:T(8,128)}, u32[]{:S(2)}) copy-start(s32[64,6]{0,1:T(8,128)} %param.16) | copy-start | bytes 4612
  624.9 57.9 %all-gather.11.cloned.1.call-start = ((), (), s32[]{:S(2)}) async-start(), calls=%async_computation.10 | async-start | bytes 1310720 | tf_op jit(solution)/shard_map/all_gather | solution.py:117
  640.2 15.1 %copy-start.2 = (bf16[64,2048]{1,0:T(8,128)(2,1)S(1)}, bf16[64,2048]{1,0:T(8,128)(2,1)}, u32[]{:S(2)}) copy-start(bf16[64,2048]{1,0:T(8,128)(2,1)} %param.11) | copy-start | bytes 786436
  640.2 16.3 %copy-start.9 = (f32[2048]{0:T(1024)S(1)}, f32[2048]{0:T(1024)}, u32[]{:S(2)}) copy-start(f32[2048]{0:T(1024)} %param.20) | copy-start | bytes 24580
  656.5 28.7 %copy-start.4 = (bf16[64,2048]{1,0:T(8,128)(2,1)}, bf16[64,2048]{1,0:T(8,128)(2,1)S(1)}, u32[]{:S(2)}) copy-start(bf16[64,2048]{1,0:T(8,128)(2,1)S(1)} %get-tuple-element.3) | copy-start | bytes 786436
Sparse Core Ops, SparseCore 0:
  144.1 168.7 all-gather.6
  341.7 118.1 reduce-scatter.2
  462.3 25.2 all-gather.8
  489.3 123.3 all-gather.12
  625.1 30.1 reduce-scatter.4
  657.5 25.2 all-gather.10
where the time goes:
time: 702 us; the launch traced here: 692 us
  waiting for transfers between devices  399 us (57%)
  blocking collectives  126 us (18%)
  local copies, waits for them, and re-layouts  70.2 us (10%)
  matrix products  43.2 us (6%)
  starting transfers between devices  25 us (4%)
  between operations  14.6 us (2%)
  other arithmetic  14.5 us (2%)
    all_gather x1, waiting for transfers between devices, on_device(): shared_cat = lax.all_gather(shared_cat, 'expert', axis=1, tiled=False)  125 us
    all_to_all x1, blocking collectives, on_device(): lax.all_to_all(send.reshape(n_groups, capacity, width), ('dp', 'expert'),...  109 us
    reduce_scatter x1, waiting for transfers between devices, on_device(): lax.psum_scatter(expert_part(rows, gate_up_w, down_w).astype(jnp.bfloat16...  100 us
    all_gather x1, waiting for transfers between devices, on_device(): every_slot = lax.all_gather(slots_here, 'mp', axis=0, tiled=True)  70.8 us
    all_to_all x1, waiting for transfers between devices, on_device(): lax.all_to_all(in_send, ('expert', 'mp'), split_axis=0, concat_axis=1, ti...  54.8 us
    all_gather x1, waiting for transfers between devices, on_device(): next_group = lax.all_gather(next_rows, 'mp', axis=0, tiled=True)  25.5 us
    all_gather x1, blocking collectives, on_device(): shared_cat = lax.all_gather(shared_cat, 'dp', axis=0, tiled=False)  17.1 us
    dot_general x1, matrix products, expert_part(): gate_up = jnp.dot(rows, gate_up_w, preferred_element_type=jnp.float32)  15.1 us
  transfers between devices with their start and end apart: 9, of which 7 were waited for; matrix products, arithmetic and copies ran while one was open for 12% of the time, Pallas kernels for 0%

commit v1 on v0

--- a/solution.py
+++ b/solution.py
@@ -2,6 +2,11 @@
 import jax.numpy as jnp
 from jax import lax
 from jax.sharding import PartitionSpec as P
+
+
+def gather_over(x, name, along):
+    stack = jnp.stack([x] * lax.axis_size(name))
+    return jnp.concatenate(lax.all_to_all(stack, name, 0, 0), axis=along)
 
 
 def rms_scale(values, gain):
@@ -79,7 +84,7 @@
         tiled=True,
     )
     slots_here = received.reshape(n_groups * capacity, width)
-    every_slot = lax.all_gather(slots_here, "mp", axis=0, tiled=True)
+    every_slot = gather_over(slots_here, "mp", 0)
     rows = every_slot
     summed = lax.psum_scatter(
         expert_part(rows, gate_up_w, down_w).astype(jnp.bfloat16),

time: 702 us -> 745 us (1.061)
  waiting for transfers between devices: 399 us -> 525 us
  blocking collectives: 126 us -> 13.5 us
  starting transfers between devices: 25 us -> 47.1 us
  local copies, waits for them, and re-layouts: 70.2 us -> 77.8 us
    all_to_all x0 -> x2, waiting for transfers between devices: none -> 218 us  [the longest x1 137 us: gather_over(): return jnp.concatenate(lax.all_to_all(stack, name, 0, 0), axis=along)]
    all_to_all x1 -> x0, blocking collectives: 109 us -> none  [on_device(): lax.all_to_all(send.reshape(n_groups, capacity, width), ('dp', 'expert'),...]
    all_gather x1 -> x0, waiting for transfers between devices: 70.8 us -> none  [on_device(): every_slot = lax.all_gather(slots_here, 'mp', axis=0, tiled=True)]
    all_to_all x0 -> x2, starting transfers between devices: none -> 20.6 us  [the longest x1 14 us: on_device(): lax.all_to_all(send.reshape(n_groups, capacity, width), ('dp', 'expert'),...]
    all_to_all x1, waiting for transfers between devices: 54.8 us -> 34.6 us  [on_device(): lax.all_to_all(in_send, ('expert', 'mp'), split_axis=0, concat_axis=1, ti...]
    another operation x1 -> x3, local copies, waits for them, and re-layouts: 0.48 us -> 14.8 us  [the longest x2 14.3 us: gather_over(): stack = jnp.stack([x] * lax.axis_size(name))]
  transfers between devices with their start and end apart: 9 -> 10, of which waited for: 7 -> 8; matrix products, arithmetic and copies ran while one was open for 12% -> 12% of each run, Pallas kernels for 0% -> 0%
where the time goes in v1:
time: 745 us; the launch traced here: 736 us
  waiting for transfers between devices  525 us (70%)
  local copies, waits for them, and re-layouts  77.8 us (10%)
  starting transfers between devices  47.1 us (6%)
  matrix products  43.2 us (6%)
  other arithmetic  14.6 us (2%)
  between operations  14.3 us (2%)
  blocking collectives  13.5 us (2%)
    all_to_all x1, waiting for transfers between devices, gather_over(): return jnp.concatenate(lax.all_to_all(stack, name, 0, 0), axis=along)  137 us
    all_gather x1, waiting for transfers between devices, on_device(): shared_cat = lax.all_gather(shared_cat, 'expert', axis=1, tiled=False)  125 us
    reduce_scatter x1, waiting for transfers between devices, on_device(): lax.psum_scatter(expert_part(rows, gate_up_w, down_w).astype(jnp.bfloat16...  99.9 us
    all_to_all x1, waiting for transfers between devices, on_device(): lax.all_to_all(send.reshape(n_groups, capacity, width), ('dp', 'expert'),...  81.4 us
    all_to_all x1, waiting for transfers between devices, on_device(): lax.all_to_all(in_send, ('expert', 'mp'), split_axis=0, concat_axis=1, ti...  34.6 us
    all_gather x1, waiting for transfers between devices, on_device(): next_group = lax.all_gather(next_rows, 'mp', axis=0, tiled=True)  25.5 us
    dot_general x1, matrix products, expert_part(): gate_up = jnp.dot(rows, gate_up_w, preferred_element_type=jnp.float32)  15.2 us
  transfers between devices with their start and end apart: 10, of which 8 were waited for; matrix products, arithmetic and copies ran while one was open for 12% of the time, Pallas kernels for 0%

profile of v1, /device:TPU:1, one launch (start us, length us, event | category | flops | bytes accessed | tf_op | source)
XLA Modules:
  0.0 735.9 jit_solution(16102995361787878350)
XLA Ops:
  12.8 10.0 %scatter_custom_fusion = bf16[768,2048]{1,0:T(8,128)(2,1)} fusion(s32[384]{0:T(512)S(1)} %fusion.38, bf16[64,2048]{1,0:T(8,128)(2,1)S(1)} %fusion.30, s32[1024]{0:T(1024)S(1)} %pad_clamp_fusion.1, bf16[]{:T(256)} %constant.12.clone.1), kind=kCustom, calls=%fused_computation.15 | custom fusion | bytes 3145730 | tf_op jit(solution)/shard_map/scatter | solution.py:77
  22.8 6.1 reshape.158
  28.9 14.0 %all-to-all-start = ((bf16[64,12,2048]{2,1,0:T(8,128)(2,1)}), bf16[64,12,2048]{2,1,0:T(8,128)(2,1)}, u32[]{:S(2)}, u32[]{:S(2)}) async-start(bf16[64,12,2048]{2,1,0:T(8,128)(2,1)} %reshape.158), calls=%async_computation | async-start | bytes 8388608 | tf_op jit(solution)/shard_map/all_to_all | solution.py:79
  55.3 81.4 %all-to-all-done = bf16[64,12,2048]{2,1,0:T(8,128)(2,1)} async-done(((bf16[64,12,2048]{2,1,0:T(8,128)(2,1)}), bf16[64,12,2048]{2,1,0:T(8,128)(2,1)}, u32[]{:S(2)}, u32[]{:S(2)}) %all-to-all-start) | async-done | bytes 3145760 | tf_op jit(solution)/shard_map/all_to_all | solution.py:79
  136.7 10.1 %all-to-all-start.2 = ((bf16[64,32,2,352]{3,1,2,0:T(8,128)(2,1)}), bf16[64,32,2,352]{3,1,2,0:T(8,128)(2,1)}, u32[]{:S(2)}, u32[]{:S(2)}) async-start(bf16[64,32,2,352]{3,1,2,0:T(8,128)(2,1)} %bitcast.34), calls=%async_computation.2 | async-start | bytes 6291456 | tf_op jit(solution)/shard_map/all_to_all | solution.py:61
  146.9 6.2 stack_reshape.2
  153.0 34.6 %all-to-all-done.2 = bf16[64,32,2,352]{3,1,2,0:T(8,128)(2,1)} async-done(((bf16[64,32,2,352]{3,1,2,0:T(8,128)(2,1)}), bf16[64,32,2,352]{3,1,2,0:T(8,128)(2,1)}, u32[]{:S(2)}, u32[]{:S(2)}) %all-to-all-start.2) | async-done | bytes 2883616 | tf_op jit(solution)/shard_map/all_to_all | solution.py:61
  187.6 8.1 %stack.3 = bf16[4,768,2048]{2,1,0:T(8,128)(2,1)} broadcast(bf16[768,2048]{1,0:T(8,128)(2,1)} %stack_reshape.2), dimensions={1,2} | broadcast | bytes 15728640 | tf_op jit(solution)/shard_map/stack | solution.py:8
  195.8 6.6 all-to-all-start.1
  204.4 136.6 %all-to-all-done.1 = bf16[4,768,2048]{2,1,0:T(8,128)(2,1)} async-done(((bf16[4,768,2048]{2,1,0:T(8,128)(2,1)}), bf16[4,768,2048]{2,1,0:T(8,128)(2,1)}, u32[]{:S(2)}, u32[]{:S(2)}) %all-to-all-start.1) | async-done | bytes 12582944 | tf_op jit(solution)/shard_map/all_to_all | solution.py:9
  346.2 6.9 copy.25
  353.1 7.8 %reshape.162 = bf16[2048,704]{1,0:T(8,128)(2,1)} reshape(bf16[64,32,2,352]{3,2,1,0:T(2,128)(2,1)} %copy.25) | data formatting | bytes 5767168 | tf_op jit(solution)/shard_map/reshape | solution.py:64
  360.9 15.2 %fusion.44 = f32[3072,704]{0,1:T(8,128)} fusion(bf16[3072,2048]{1,0:T(8,128)(2,1)} %bitcast.1, bf16[2048,704]{1,0:T(8,128)(2,1)} %reshape.162), kind=kOutput, calls=%fused_computation.67 | convolution fusion | flops 8858370048 | bytes 24117248 | tf_op jit(solution)/shard_map/dot_general | solution.py:20
  376.0 13.4 %convolution_convert_fusion = bf16[3072,2048]{1,0:T(8,128)(2,1)} fusion(bf16[2048,352]{1,0:T(8,128)(2,1)S(1)} %bitcast.37, f32[3072,704]{0,1:T(8,128)} %fusion.44), kind=kOutput, calls=%fused_computation.3 | convolution fusion | flops 4441964544 | bytes 22675456 | tf_op jit(solution)/shard_map/dot_general | solution.py:22
  390.4 13.5 %all-gather = bf16[128,2112]{1,0:T(8,128)(2,1)} all-gather(bf16[32,2112]{1,0:T(8,128)(2,1)S(1)} %concatenate.7), channel_id=2, replica_groups=mesh['dp'=4,'expert'=16,'mp'=4] {'dp'}, dimensions={0}, use_global_device_ids=true | all-gather | bytes 675840 | tf_op jit(solution)/shard_map/all_gather | solution.py:103
  403.9 99.9 %reduce-scatter.3.cloned.1.call-done = bf16[768,2048]{1,0:T(8,128)(2,1)} async-done(((bf16[3072,2048]{1,0:T(8,128)(2,1)}), bf16[768,2048]{1,0:T(8,128)(2,1)}) %reduce-scatter.3.cloned.1.call-update) | async-done | bytes 3145744 | tf_op jit(solution)/shard_map/reduce_scatter | solution.py:89
  509.9 10.8 %all-to-all-start.4 = ((bf16[64,12,2048]{2,1,0:T(8,128)(2,1)}), bf16[64,12,2048]{2,1,0:T(8,128)(2,1)}, u32[]{:S(2)}, u32[]{:S(2)}) async-start(bf16[64,12,2048]{2,1,0:T(8,128)(2,1)} %reshape.165), calls=%async_computation.5 | async-start | bytes 8388608 | tf_op jit(solution)/shard_map/all_to_all | solution.py:96
  521.0 10.5 %all-gather.6.cloned.1.call-done = bf16[256,2048]{1,0:T(8,128)(2,1)} async-done(((bf16[64,2048]{1,0:T(8,128)(2,1)}), bf16[256,2048]{1,0:T(8,128)(2,1)}) %all-gather.6.cloned.1.call-update) | async-done | bytes 1048592 | tf_op jit(solution)/shard_map/all_gather | solution.py:109
  531.6 125.0 %all-gather.10.cloned.1.call-done = bf16[4,512,2112]{2,1,0:T(8,128)(2,1)} async-done(((bf16[4,32,2112]{2,1,0:T(8,128)(2,1)}), bf16[4,512,2112]{2,1,0:T(8,128)(2,1)}) %all-gather.10.cloned.1.call-update) | async-done | bytes 8650768 | tf_op jit(solution)/shard_map/all_gather | solution.py:104
  660.1 8.8 %fusion.1 = f32[256,2048]{1,0:T(8,128)} fusion(bf16[2048,2112]{1,0:T(8,128)(2,1)} %bitcast.40, bf16[256,2048]{1,0:T(8,128)(2,1)S(1)} %copy-done.10, f32[256,704]{0,1:T(8,128)S(1)} %fusion.5), kind=kOutput, calls=%fused_computation.7 | convolution fusion | flops 1477476352 | bytes 10158080 | tf_op jit(solution)/shard_map/dot_general | solution.py:115
  669.1 6.2 reshape.166
  675.3 6.7 gather_fusion
  688.0 11.2 %reduce-scatter.5.cloned.1.call-done = f32[64,2048]{1,0:T(8,128)} async-done(((f32[256,2048]{1,0:T(8,128)}), f32[64,2048]{1,0:T(8,128)}) %reduce-scatter.5.cloned.1.call-update) | async-done | bytes 524304 | tf_op jit(solution)/shard_map/reduce_scatter | solution.py:114
  701.4 25.5 %all-gather.8.cloned.1.call-done = bf16[256,2048]{1,0:T(8,128)(2,1)} async-done(((bf16[64,2048]{1,0:T(8,128)(2,1)}), bf16[256,2048]{1,0:T(8,128)(2,1)}) %all-gather.8.cloned.1.call-update) | async-done | bytes 1048592 | tf_op jit(solution)/shard_map/all_gather | solution.py:122
  (71 shorter events, 46.8 us)
Async XLA Ops:
  7.2 719.7 %copy-start = (bf16[2048,144]{0,1:T(8,128)(2,1)S(1)}, bf16[2048,144]{0,1:T(8,128)(2,1)}, u32[]{:S(2)}) copy-start(bf16[2048,144]{0,1:T(8,128)(2,1)} %param.21) | copy-start | bytes 1769476
  12.8 16.1 %copy-start.3 = (bf16[64,2048]{1,0:T(8,128)(2,1)}, bf16[64,2048]{1,0:T(8,128)(2,1)S(1)}, u32[]{:S(2)}) copy-start(bf16[64,2048]{1,0:T(8,128)(2,1)S(1)} %fusion.30) | copy-start | bytes 786436
  28.9 107.9 %all-to-all-start = ((bf16[64,12,2048]{2,1,0:T(8,128)(2,1)}), bf16[64,12,2048]{2,1,0:T(8,128)(2,1)}, u32[]{:S(2)}, u32[]{:S(2)}) async-start(bf16[64,12,2048]{2,1,0:T(8,128)(2,1)} %reshape.158), calls=%async_computation | async-start | bytes 8388608 | tf_op jit(solution)/shard_map/all_to_all | solution.py:79
  136.7 50.9 %all-to-all-start.2 = ((bf16[64,32,2,352]{3,1,2,0:T(8,128)(2,1)}), bf16[64,32,2,352]{3,1,2,0:T(8,128)(2,1)}, u32[]{:S(2)}, u32[]{:S(2)}) async-start(bf16[64,32,2,352]{3,1,2,0:T(8,128)(2,1)} %bitcast.34), calls=%async_computation.2 | async-start | bytes 6291456 | tf_op jit(solution)/shard_map/all_to_all | solution.py:61
  195.7 6.6 copy-start.1
  195.8 145.3 %all-to-all-start.1 = ((bf16[4,768,2048]{2,1,0:T(8,128)(2,1)}), bf16[4,768,2048]{2,1,0:T(8,128)(2,1)}, u32[]{:S(2)}, u32[]{:S(2)}) async-start(bf16[4,768,2048]{2,1,0:T(8,128)(2,1)} %stack.3), calls=%async_computation.1 | async-start | bytes 25165824 | tf_op jit(solution)/shard_map/all_to_all | solution.py:9
  341.0 35.0 %all-to-all-start.3 = ((bf16[64,32,352]{2,1,0:T(8,128)(2,1)}), bf16[64,32,352]{2,1,0:T(8,128)(2,1)S(1)}, u32[]{:S(2)}, u32[]{:S(2)}) async-start(bf16[64,32,352]{2,1,0:T(8,128)(2,1)} %bitcast.4), calls=%async_computation.3 | async-start | bytes 3145728 | tf_op jit(solution)/shard_map/all_to_all | solution.py:62
  346.2 157.6 %reduce-scatter.3.cloned.1.call-start = ((), (), s32[]{:S(2)}) async-start(), calls=%async_computation.7 | async-start | bytes 15728640 | tf_op jit(solution)/shard_map/reduce_scatter | solution.py:89
  389.5 0.8 copy-start.5
  389.5 0.8 copy-start.6
  389.5 0.8 copy-start.7
  389.5 142.1 %all-gather.6.cloned.1.call-start = ((), (), s32[]{:S(2)}) async-start(), calls=%async_computation.8 | async-start | bytes 1310720 | tf_op jit(solution)/shard_map/all_gather | solution.py:109
  390.2 266.3 %all-gather.10.cloned.1.call-start = ((), (), s32[]{:S(2)}) async-start(), calls=%async_computation.11 | async-start | bytes 9469952 | tf_op jit(solution)/shard_map/all_gather | solution.py:104
  509.9 159.2 %all-to-all-start.4 = ((bf16[64,12,2048]{2,1,0:T(8,128)(2,1)}), bf16[64,12,2048]{2,1,0:T(8,128)(2,1)}, u32[]{:S(2)}, u32[]{:S(2)}) async-start(bf16[64,12,2048]{2,1,0:T(8,128)(2,1)} %reshape.165), calls=%async_computation.5 | async-start | bytes 8388608 | tf_op jit(solution)/shard_map/all_to_all | solution.py:96
  520.7 178.5 %reduce-scatter.5.cloned.1.call-start = ((), (), s32[]{:S(2)}) async-start(), calls=%async_computation.9 | async-start | bytes 2621440 | tf_op jit(solution)/shard_map/reduce_scatter | solution.py:114
  531.6 128.5 %copy-start.10 = (bf16[256,2048]{1,0:T(8,128)(2,1)S(1)}, bf16[256,2048]{1,0:T(8,128)(2,1)}, u32[]{:S(2)}) copy-start(bf16[256,2048]{1,0:T(8,128)(2,1)} %all-gather.6.cloned.1.call-done) | copy-start | bytes 3145732
  660.1 8.8 %copy-start.8 = (s32[64,6]{0,1:T(8,128)S(1)}, s32[64,6]{0,1:T(8,128)}, u32[]{:S(2)}) copy-start(s32[64,6]{0,1:T(8,128)} %param.16) | copy-start | bytes 4612
  668.9 57.9 %all-gather.8.cloned.1.call-start = ((), (), s32[]{:S(2)}) async-start(), calls=%async_computation.10 | async-start | bytes 1310720 | tf_op jit(solution)/shard_map/all_gather | solution.py:122
  684.1 15.1 %copy-start.2 = (bf16[64,2048]{1,0:T(8,128)(2,1)S(1)}, bf16[64,2048]{1,0:T(8,128)(2,1)}, u32[]{:S(2)}) copy-start(bf16[64,2048]{1,0:T(8,128)(2,1)} %param.11) | copy-start | bytes 786436
  684.1 16.4 %copy-start.9 = (f32[2048]{0:T(1024)S(1)}, f32[2048]{0:T(1024)}, u32[]{:S(2)}) copy-start(f32[2048]{0:T(1024)} %param.20) | copy-start | bytes 24580
  700.5 28.7 %copy-start.4 = (bf16[64,2048]{1,0:T(8,128)(2,1)}, bf16[64,2048]{1,0:T(8,128)(2,1)S(1)}, u32[]{:S(2)}) copy-start(bf16[64,2048]{1,0:T(8,128)(2,1)S(1)} %get-tuple-element.3) | copy-start | bytes 786436
Sparse Core Ops, SparseCore 0:
  389.6 114.1 reduce-scatter.2
  506.2 25.3 all-gather.5
  533.4 123.1 all-gather.9
  669.0 30.1 reduce-scatter.4
  701.5 25.2 all-gather.7
